TPU v7x, 32 devices: a whole 2x2x4 slice. The times are simulated.
32 devices in a mesh: grad: 4 (over y, x), col: 8 (over z, core).
Axes of the slice: x: 2, y: 2, z: 4, core: 2. Of those that a mesh axis runs over, the one named last changes fastest.
Arguments:
- gradient: bfloat16 [16384, 53248], P(('grad', 'col'))
- test_matrix: bfloat16 [16384, 256], P(('grad', 'col')), may hold values from -6 to 6
Outputs:
- low_rank: float32 [16384, 256], P(('grad', 'col'))
- projector: float32 [53248, 256], P('col')
All inputs are finite; a program needn't handle non-finite values.
Results may differ from a plain program's by a relative error of at most 0.008.
Values may be sent and summed in bfloat16 or wider, within the bound.
No kernel may reach another device: no remote copies, remote signals or barrier semaphores. Data moves between devices by JAX's collectives and lax.ppermute only.
A program may use at most 256 MiB of HBM per device.

v0:
```python
import math
import jax
import jax.numpy as jnp
from jax import lax
from jax.sharding import PartitionSpec as P

FF = 53248
POWER = 2


def orthonormal(matrix, reduce_gram):
    partial_gram = lax.dot_general(
        matrix,
        matrix,
        (((0,), (0,)), ((), ())),
        precision=lax.Precision.HIGHEST,
        preferred_element_type=jnp.float32,
    )
    gram = reduce_gram(partial_gram)
    lower_factor = jnp.linalg.cholesky(gram)
    return lax.linalg.triangular_solve(
        lower_factor, matrix, left_side=False, lower=True, transpose_a=True
    )


def gram_over_columns(partial_gram):
    return lax.psum(partial_gram, "col")


def shards(gradient, test_matrix):
    blocks = lax.all_to_all(gradient, "col", split_axis=1, concat_axis=0, tiled=True)

    def add_sketch(row_piece):
        return lax.dot_general(
            blocks, row_piece, (((0,), (0,)), ((), ())), preferred_element_type=jnp.float32
        )

    sketch = add_sketch(lax.all_gather(test_matrix, "col", axis=0, tiled=True))
    for iteration in range(POWER + 1):
        summed = lax.psum(sketch, "grad")
        basis_block = orthonormal(summed, gram_over_columns)
        basis_bf = basis_block.astype(jnp.bfloat16)
        reduced = lax.psum_scatter(
            jnp.dot(blocks, basis_bf, preferred_element_type=jnp.float32),
            "col",
            scatter_dimension=0,
            tiled=True,
        )
        if iteration < POWER:
            reduced_bf = reduced.astype(jnp.bfloat16)
            sketch = add_sketch(lax.all_gather(reduced_bf, "col", axis=0, tiled=True))
    return (reduced, basis_block * math.sqrt(FF))


def solution(mesh):
    return jax.shard_map(
        shards,
        mesh=mesh,
        in_specs=(P(("grad", "col"), None), P(("grad", "col"), None)),
        out_specs=(P(("grad", "col"), None), P("col", None)),
        check_vma=False,
    )
```

profile of v0, /device:TPU:0, one launch (start us, length us, event | category | flops | bytes accessed | tf_op | source)
XLA Modules:
  0.0 2602.8 jit_solution(11232503956803364355)
XLA Ops:
  7.2 70.6 %copy.20 = bf16[512,53248]{0,1:T(8,128)(2,1)} copy(bf16[512,53248]{1,0:T(8,128)(2,1)} %param.5) | data formatting | bytes 109051904 | tf_op args[0]
  77.8 8.8 all-to-all-start
  87.4 1189.5 %all-to-all-done = bf16[512,8,6656]{0,2,1:T(8,128)(2,1)} async-done(((bf16[512,8,6656]{0,2,1:T(8,128)(2,1)}), bf16[512,8,6656]{0,2,1:T(8,128)(2,1)}, u32[]{:S(2)}, u32[]{:S(2)}) %all-to-all-start) | async-done | bytes 54525984 | tf_op jit(solution)/shard_map/all_to_all | solution.py:31
  1276.9 64.6 %copy.21 = bf16[8,512,6656]{2,1,0:T(8,128)(2,1)} copy(bf16[8,512,6656]{1,2,0:T(8,128)(2,1)} %bitcast.1) | data formatting | bytes 109051904 | tf_op jit(solution)/shard_map/all_to_all | solution.py:31
  1341.5 25.8 fusion.41
  1367.7 146.1 %all-reduce.8.cloned.1.call-done = f32[6656,256]{1,0:T(8,128)} async-done(((f32[6656,256]{1,0:T(8,128)}), f32[6656,256]{1,0:T(8,128)}) %all-reduce.8.cloned.1.call-update) | async-done | bytes 6815760 | tf_op jit(solution)/shard_map/psum | solution.py:40
  1513.8 16.6 fusion.42
  1531.0 55.0 %all-reduce.10.cloned.1.call-done = f32[256,256]{0,1:T(8,128)} async-done(((f32[256,256]{0,1:T(8,128)}), f32[256,256]{0,1:T(8,128)}) %all-reduce.10.cloned.1.call-update) | async-done | bytes 262160 | tf_op jit(solution)/shard_map/psum | solution.py:27
  1586.0 1.1 copy.23
  1587.1 1.0 fusion.11
  1588.1 11.7 cholesky.172
  1599.8 9.8 custom-call.15
  1610.2 11.7 cholesky.189
  1624.0 4.2 while.6
  1624.8 1.4 bitcast_dynamic-update-slice_fusion.6
  1626.8 1.4 bitcast_dynamic-update-slice_fusion.6
  1628.9 19.7 custom-call.16
  1648.5 5.2 fusion.7
  1653.7 6.5 convolution_subtract_fusion.2
  1660.3 4.5 fusion.20
  1664.7 24.3 convolution_bitcast_fusion.4
  1689.1 49.1 %reduce-scatter.4.cloned.1.call-done = f32[512,256]{0,1:T(8,128)} async-done(((f32[4096,256]{0,1:T(8,128)}), f32[512,256]{0,1:T(8,128)}) %reduce-scatter.4.cloned.1.call-update) | async-done | bytes 524304 | tf_op jit(solution)/shard_map/reduce_scatter | solution.py:43
  1738.2 1.8 convert_element_type.16
  1740.1 27.8 %all-gather.6.cloned.1.call-done = bf16[4096,256]{0,1:T(8,128)(2,1)} async-done(((bf16[512,256]{0,1:T(8,128)(2,1)}), bf16[4096,256]{0,1:T(8,128)(2,1)}) %all-gather.6.cloned.1.call-update) | async-done | bytes 2097168 | tf_op jit(solution)/shard_map/all_gather | solution.py:51
  1767.9 25.5 convolution_bitcast_fusion.1
  1793.5 146.3 %all-reduce.12.cloned.1.call-done = f32[6656,256]{0,1:T(8,128)} async-done(((f32[6656,256]{0,1:T(8,128)}), f32[6656,256]{0,1:T(8,128)}) %all-reduce.12.cloned.1.call-update) | async-done | bytes 6815760 | tf_op jit(solution)/shard_map/psum | solution.py:40
  1939.8 19.3 fusion.43
  1959.6 55.1 %all-reduce.14.cloned.1.call-done = f32[256,256]{0,1:T(8,128)} async-done(((f32[256,256]{0,1:T(8,128)}), f32[256,256]{0,1:T(8,128)}) %all-reduce.14.cloned.1.call-update) | async-done | bytes 262160 | tf_op jit(solution)/shard_map/psum | solution.py:27
  2014.7 1.1 copy.25
  2016.8 11.7 cholesky.206
  2028.6 9.8 custom-call.17
  2038.9 11.7 cholesky.223
  2053.2 4.2 while.7
  2054.0 1.4 bitcast_dynamic-update-slice_fusion.7
  2056.0 1.4 bitcast_dynamic-update-slice_fusion.7
  2058.1 19.7 custom-call.18
  2077.8 5.2 fusion.5
  2083.0 4.2 convolution_subtract_fusion.1
  2087.2 4.3 fusion.16
  2091.4 24.5 convolution_bitcast_fusion.3
  2116.0 49.1 %reduce-scatter.6.cloned.1.call-done = f32[512,256]{0,1:T(8,128)} async-done(((f32[4096,256]{0,1:T(8,128)}), f32[512,256]{0,1:T(8,128)}) %reduce-scatter.6.cloned.1.call-update) | async-done | bytes 524304 | tf_op jit(solution)/shard_map/reduce_scatter | solution.py:43
  2165.1 1.8 convert_element_type.18
  2167.0 28.0 %all-gather.8.cloned.1.call-done = bf16[4096,256]{0,1:T(8,128)(2,1)} async-done(((bf16[512,256]{0,1:T(8,128)(2,1)}), bf16[4096,256]{0,1:T(8,128)(2,1)}) %all-gather.8.cloned.1.call-update) | async-done | bytes 2097168 | tf_op jit(solution)/shard_map/all_gather | solution.py:51
  2194.9 25.5 convolution_bitcast_fusion
  2220.5 146.3 %all-reduce.16.cloned.1.call-done = f32[6656,256]{0,1:T(8,128)} async-done(((f32[6656,256]{0,1:T(8,128)}), f32[6656,256]{0,1:T(8,128)}) %all-reduce.16.cloned.1.call-update) | async-done | bytes 6815760 | tf_op jit(solution)/shard_map/psum | solution.py:40
  2366.8 19.3 fusion.44
  2386.6 55.1 %all-reduce.18.cloned.1.call-done = f32[256,256]{0,1:T(8,128)} async-done(((f32[256,256]{0,1:T(8,128)}), f32[256,256]{0,1:T(8,128)}) %all-reduce.18.cloned.1.call-update) | async-done | bytes 262160 | tf_op jit(solution)/shard_map/psum | solution.py:27
  2441.8 1.1 copy.28
  2442.9 1.0 fusion.9
  2443.9 11.7 cholesky.240
  2455.6 9.8 custom-call.19
  2465.9 11.7 cholesky.257
  2480.3 4.2 while.8
  2481.1 1.4 bitcast_dynamic-update-slice_fusion.8
  2483.1 1.4 bitcast_dynamic-update-slice_fusion.8
  2485.2 19.7 custom-call.20
  2504.9 5.2 fusion.3
  2510.0 4.2 convolution_subtract_fusion
  2514.2 4.9 fusion.12
  2519.2 25.4 convolution_bitcast_fusion.2
  2544.6 5.4 fusion
  2549.9 8.1 copy.31
  2558.0 35.7 %reduce-scatter.8.cloned.1.call-done = f32[512,256]{0,1:T(8,128)} async-done(((f32[4096,256]{0,1:T(8,128)}), f32[512,256]{0,1:T(8,128)}) %reduce-scatter.8.cloned.1.call-update) | async-done | bytes 524304 | tf_op jit(solution)/shard_map/reduce_scatter | solution.py:43
  2593.7 2.0 copy.30
  (81 shorter events, 14.8 us)
Async XLA Ops:
  77.8 1199.1 %all-to-all-start = ((bf16[512,8,6656]{0,2,1:T(8,128)(2,1)}), bf16[512,8,6656]{0,2,1:T(8,128)(2,1)}, u32[]{:S(2)}, u32[]{:S(2)}) async-start(bf16[512,8,6656]{0,2,1:T(8,128)(2,1)} %bitcast.124), calls=%async_computation | async-start | bytes 109051904 | tf_op jit(solution)/shard_map/all_to_all | solution.py:31
  86.6 1254.9 %all-gather.4.cloned.1.call-start = ((), (), s32[]{:S(2)}) async-start(), calls=%async_computation.4 | async-start | bytes 2359296 | tf_op jit(solution)/shard_map/all_gather | solution.py:38
  87.3 1426.5 %all-reduce.8.cloned.1.call-start = ((), (), s32[]{:S(2)}) async-start(), calls=%async_computation.5 | async-start | bytes 13631488 | tf_op jit(solution)/shard_map/psum | solution.py:40
  1367.4 218.6 %all-reduce.10.cloned.1.call-start = ((), (), s32[]{:S(2)}) async-start(), calls=%async_computation.6 | async-start | bytes 524288 | tf_op jit(solution)/shard_map/psum | solution.py:27
  1530.4 207.8 %reduce-scatter.4.cloned.1.call-start = ((), (), s32[]{:S(2)}) async-start(), calls=%async_computation.7 | async-start | bytes 4718592 | tf_op jit(solution)/shard_map/reduce_scatter | solution.py:43
  1628.2 0.7 copy-start.4
  1648.5 5.2 copy-start
  1689.1 78.8 %all-gather.6.cloned.1.call-start = ((), (), s32[]{:S(2)}) async-start(), calls=%async_computation.8 | async-start | bytes 2359296 | tf_op jit(solution)/shard_map/all_gather | solution.py:51
  1740.0 199.8 %all-reduce.12.cloned.1.call-start = ((), (), s32[]{:S(2)}) async-start(), calls=%async_computation.9 | async-start | bytes 13631488 | tf_op jit(solution)/shard_map/psum | solution.py:40
  1793.4 221.3 %all-reduce.14.cloned.1.call-start = ((), (), s32[]{:S(2)}) async-start(), calls=%async_computation.10 | async-start | bytes 524288 | tf_op jit(solution)/shard_map/psum | solution.py:27
  1959.1 206.0 %reduce-scatter.6.cloned.1.call-start = ((), (), s32[]{:S(2)}) async-start(), calls=%async_computation.11 | async-start | bytes 4718592 | tf_op jit(solution)/shard_map/reduce_scatter | solution.py:43
  2057.4 0.7 copy-start.5
  2077.8 5.2 copy-start.2
  2116.0 79.0 %all-gather.8.cloned.1.call-start = ((), (), s32[]{:S(2)}) async-start(), calls=%async_computation.12 | async-start | bytes 2359296 | tf_op jit(solution)/shard_map/all_gather | solution.py:51
  2166.9 199.9 %all-reduce.16.cloned.1.call-start = ((), (), s32[]{:S(2)}) async-start(), calls=%async_computation.13 | async-start | bytes 13631488 | tf_op jit(solution)/shard_map/psum | solution.py:40
  2220.5 221.3 %all-reduce.18.cloned.1.call-start = ((), (), s32[]{:S(2)}) async-start(), calls=%async_computation.14 | async-start | bytes 524288 | tf_op jit(solution)/shard_map/psum | solution.py:27
  2386.2 207.5 %reduce-scatter.8.cloned.1.call-start = ((), (), s32[]{:S(2)}) async-start(), calls=%async_computation.15 | async-start | bytes 4718592 | tf_op jit(solution)/shard_map/reduce_scatter | solution.py:43
  2484.5 0.7 copy-start.3
  2504.9 5.2 copy-start.1
Sparse Core Ops, SparseCore 0:
  89.0 49.5 all-gather.3
  1367.5 146.2 all-reduce.7
  1530.6 55.4 all-reduce.9
  1689.2 48.9 reduce-scatter.3
  1740.2 27.5 all-gather.5
  1793.5 146.1 all-reduce.11
  1959.2 55.4 all-reduce.13
  2116.1 48.9 reduce-scatter.5
  2167.3 27.6 all-gather.7
  2220.6 146.1 all-reduce.15
  2386.3 55.4 all-reduce.17
  2544.7 48.9 reduce-scatter.7
where the time goes:
time: 2610 us; the launch traced here: 2600 us
  waiting for transfers between devices  1980 us (76%)
  matrix products  252 us (10%)
  other arithmetic  174 us (7%)
  local copies, waits for them, and re-layouts  163 us (6%)
    all_to_all x1, waiting for transfers between devices, shards(): lax.all_to_all(gradient, 'col', split_axis=1, concat_axis=0, tiled=True)  1190 us
    psum x3, waiting for transfers between devices, shards(): summed = lax.psum(sketch, 'grad')  439 us
    psum x3, waiting for transfers between devices, gram_over_columns(): return lax.psum(partial_gram, 'col')  165 us
    reduce_scatter x3, waiting for transfers between devices, shards(): lax.psum_scatter(jnp.dot(blocks, basis_bf, preferred_element_type=jnp.flo...  134 us
    another operation x20, other arithmetic, orthonormal(): lower_factor = jnp.linalg.cholesky(gram)  103 us
    unnamed x15, local copies, waits for them, and re-layouts  82.9 us
    dot_general x3, matrix products, add_sketch(): lax.dot_general(blocks, row_piece, (((0,), (0,)), ((), ())), preferred_el...  76.9 us
    dot_general x3, matrix products, shards(): jnp.dot(blocks, basis_bf, preferred_element_type=jnp.float32)  74.2 us
  transfers between devices with their start and end apart: 13, of which 12 were waited for; matrix products, arithmetic and copies ran while one was open for 3% of the time, Pallas kernels for 0%

commit v1 on v0

--- a/solution.py
+++ b/solution.py
@@ -24,7 +24,7 @@
 
 
 def gram_over_columns(partial_gram):
-    return lax.psum(partial_gram, "col")
+    return jnp.sum(lax.all_gather(partial_gram, "col"), axis=0)
 
 
 def shards(gradient, test_matrix):

time: 2610 us -> 2530 us (0.969)
  waiting for transfers between devices: 1980 us -> 1910 us
    psum x3 -> x0, waiting for transfers between devices: 165 us -> none  [gram_over_columns(): return lax.psum(partial_gram, 'col')]
    all_gather x0 -> x3, waiting for transfers between devices: none -> 86.4 us  [gram_over_columns(): return jnp.sum(lax.all_gather(partial_gram, 'col'), axis=0)]
where the time goes in v1:
time: 2530 us; the launch traced here: 2520 us
  waiting for transfers between devices  1910 us (75%)
  matrix products  251 us (10%)
  other arithmetic  176 us (7%)
  local copies, waits for them, and re-layouts  160 us (6%)
    all_to_all x1, waiting for transfers between devices, shards(): lax.all_to_all(gradient, 'col', split_axis=1, concat_axis=0, tiled=True)  1190 us
    psum x3, waiting for transfers between devices, shards(): summed = lax.psum(sketch, 'grad')  439 us
    reduce_scatter x3, waiting for transfers between devices, shards(): lax.psum_scatter(jnp.dot(blocks, basis_bf, preferred_element_type=jnp.flo...  135 us
    another operation x20, other arithmetic, orthonormal(): lower_factor = jnp.linalg.cholesky(gram)  103 us
    all_gather x3, waiting for transfers between devices, gram_over_columns(): return jnp.sum(lax.all_gather(partial_gram, 'col'), axis=0)  86.4 us
    unnamed x15, local copies, waits for them, and re-layouts  82.9 us
    dot_general x3, matrix products, add_sketch(): lax.dot_general(blocks, row_piece, (((0,), (0,)), ((), ())), preferred_el...  76.9 us
    dot_general x3, matrix products, shards(): jnp.dot(blocks, basis_bf, preferred_element_type=jnp.float32)  74.2 us
  transfers between devices with their start and end apart: 13, of which 12 were waited for; matrix products, arithmetic and copies ran while one was open for 3% of the time, Pallas kernels for 0%

profile of v1, /device:TPU:0, one launch (start us, length us, event | category | flops | bytes accessed | tf_op | source)
XLA Modules:
  0.0 2524.1 jit_solution(8219104100991157887)
XLA Ops:
  7.2 70.6 %copy.23 = bf16[512,53248]{0,1:T(8,128)(2,1)} copy(bf16[512,53248]{1,0:T(8,128)(2,1)} %param.5) | data formatting | bytes 109051904 | tf_op args[0]
  77.8 8.8 all-to-all-start
  87.4 1189.5 %all-to-all-done = bf16[512,8,6656]{0,2,1:T(8,128)(2,1)} async-done(((bf16[512,8,6656]{0,2,1:T(8,128)(2,1)}), bf16[512,8,6656]{0,2,1:T(8,128)(2,1)}, u32[]{:S(2)}, u32[]{:S(2)}) %all-to-all-start) | async-done | bytes 54525984 | tf_op jit(solution)/shard_map/all_to_all | solution.py:31
  1276.9 64.6 %copy.24 = bf16[8,512,6656]{2,1,0:T(8,128)(2,1)} copy(bf16[8,512,6656]{1,2,0:T(8,128)(2,1)} %bitcast.1) | data formatting | bytes 109051904 | tf_op jit(solution)/shard_map/all_to_all | solution.py:31
  1341.5 25.8 %fusion.41 = f32[6656,256]{1,0:T(8,128)} fusion(bf16[4096,6656]{1,0:T(8,128)(2,1)} %bitcast.128, bf16[4096,256]{1,0:T(8,128)(2,1)} %all-gather.10.cloned.1.call-done), kind=kOutput, calls=%fused_computation.93 | convolution fusion | flops 13958643712 | bytes 63438848 | tf_op jit(solution)/shard_map/dot_general | solution.py:34
  1367.7 146.1 %all-reduce.5.cloned.1.call-done = f32[6656,256]{1,0:T(8,128)} async-done(((f32[6656,256]{1,0:T(8,128)}), f32[6656,256]{1,0:T(8,128)}) %all-reduce.5.cloned.1.call-update) | async-done | bytes 6815760 | tf_op jit(solution)/shard_map/psum | solution.py:40
  1513.8 16.0 fusion.42
  1530.4 28.7 %all-gather.16.cloned.1.call-done = f32[2048,256]{1,0:T(8,128)} async-done(((f32[256,256]{1,0:T(8,128)}), f32[2048,256]{1,0:T(8,128)}) %all-gather.16.cloned.1.call-update) | async-done | bytes 2097168 | tf_op jit(solution)/shard_map/all_gather | solution.py:27
  1559.2 1.8 reduce_sum.27
  1561.1 11.7 cholesky.172
  1572.9 9.8 custom-call.15
  1583.2 11.7 cholesky.189
  1597.0 4.2 while.6
  1597.8 1.4 bitcast_dynamic-update-slice_fusion.6
  1599.8 1.4 bitcast_dynamic-update-slice_fusion.6
  1601.9 19.7 custom-call.16
  1621.6 5.2 fusion.7
  1626.8 6.5 convolution_subtract_fusion.2
  1633.3 4.5 fusion.20
  1637.8 24.3 convolution_bitcast_fusion.4
  1662.2 49.4 %reduce-scatter.4.cloned.1.call-done = f32[512,256]{0,1:T(8,128)} async-done(((f32[4096,256]{0,1:T(8,128)}), f32[512,256]{0,1:T(8,128)}) %reduce-scatter.4.cloned.1.call-update) | async-done | bytes 524304 | tf_op jit(solution)/shard_map/reduce_scatter | solution.py:43
  1711.6 1.8 convert_element_type.16
  1713.4 27.8 %all-gather.12.cloned.1.call-done = bf16[4096,256]{0,1:T(8,128)(2,1)} async-done(((bf16[512,256]{0,1:T(8,128)(2,1)}), bf16[4096,256]{0,1:T(8,128)(2,1)}) %all-gather.12.cloned.1.call-update) | async-done | bytes 2097168 | tf_op jit(solution)/shard_map/all_gather | solution.py:51
  1741.3 25.5 %convolution_bitcast_fusion.1 = f32[6656,256]{0,1:T(8,128)} fusion(bf16[4096,256]{0,1:T(8,128)(2,1)} %all-gather.12.cloned.1.call-done, bf16[4096,6656]{1,0:T(8,128)(2,1)} %bitcast.130), kind=kOutput, calls=%fused_computation.7 | convolution fusion | flops 13958643712 | bytes 63438848 | tf_op jit(solution)/shard_map/dot_general | solution.py:34
  1766.9 146.3 %all-reduce.7.cloned.1.call-done = f32[6656,256]{0,1:T(8,128)} async-done(((f32[6656,256]{0,1:T(8,128)}), f32[6656,256]{0,1:T(8,128)}) %all-reduce.7.cloned.1.call-update) | async-done | bytes 6815760 | tf_op jit(solution)/shard_map/psum | solution.py:40
  1913.2 19.3 fusion.43
  1933.0 28.8 %all-gather.18.cloned.1.call-done = f32[2048,256]{1,0:T(8,128)} async-done(((f32[256,256]{1,0:T(8,128)}), f32[2048,256]{1,0:T(8,128)}) %all-gather.18.cloned.1.call-update) | async-done | bytes 2097168 | tf_op jit(solution)/shard_map/all_gather | solution.py:27
  1961.8 1.8 reduce_sum.28
  1963.8 11.7 cholesky.206
  1975.5 9.8 custom-call.17
  1985.8 11.7 cholesky.223
  2000.2 4.2 while.7
  2001.0 1.4 bitcast_dynamic-update-slice_fusion.7
  2003.0 1.4 bitcast_dynamic-update-slice_fusion.7
  2004.4 0.7 copy-done.5
  2005.1 19.7 custom-call.18
  2024.8 5.2 fusion.5
  2029.9 4.2 convolution_subtract_fusion.1
  2034.1 4.3 fusion.16
  2038.4 24.5 convolution_bitcast_fusion.3
  2063.0 49.4 %reduce-scatter.6.cloned.1.call-done = f32[512,256]{0,1:T(8,128)} async-done(((f32[4096,256]{0,1:T(8,128)}), f32[512,256]{0,1:T(8,128)}) %reduce-scatter.6.cloned.1.call-update) | async-done | bytes 524304 | tf_op jit(solution)/shard_map/reduce_scatter | solution.py:43
  2112.4 1.8 convert_element_type.18
  2114.3 28.0 %all-gather.14.cloned.1.call-done = bf16[4096,256]{0,1:T(8,128)(2,1)} async-done(((bf16[512,256]{0,1:T(8,128)(2,1)}), bf16[4096,256]{0,1:T(8,128)(2,1)}) %all-gather.14.cloned.1.call-update) | async-done | bytes 2097168 | tf_op jit(solution)/shard_map/all_gather | solution.py:51
  2142.3 25.5 %convolution_bitcast_fusion = f32[6656,256]{0,1:T(8,128)} fusion(bf16[4096,256]{0,1:T(8,128)(2,1)} %all-gather.14.cloned.1.call-done, bf16[4096,6656]{1,0:T(8,128)(2,1)} %bitcast.132), kind=kOutput, calls=%fused_computation.6 | convolution fusion | flops 13958643712 | bytes 63438848 | tf_op jit(solution)/shard_map/dot_general | solution.py:34
  2167.9 146.3 %all-reduce.9.cloned.1.call-done = f32[6656,256]{0,1:T(8,128)} async-done(((f32[6656,256]{0,1:T(8,128)}), f32[6656,256]{0,1:T(8,128)}) %all-reduce.9.cloned.1.call-update) | async-done | bytes 6815760 | tf_op jit(solution)/shard_map/psum | solution.py:40
  2314.2 19.3 fusion.44
  2334.0 28.8 %all-gather.20.cloned.1.call-done = f32[2048,256]{1,0:T(8,128)} async-done(((f32[256,256]{1,0:T(8,128)}), f32[2048,256]{1,0:T(8,128)}) %all-gather.20.cloned.1.call-update) | async-done | bytes 2097168 | tf_op jit(solution)/shard_map/all_gather | solution.py:27
  2362.8 1.8 reduce_sum.29
  2364.8 11.7 cholesky.240
  2376.5 9.8 custom-call.19
  2386.8 11.7 cholesky.257
  2401.2 4.2 while.8
  2402.0 1.4 bitcast_dynamic-update-slice_fusion.8
  2404.0 1.4 bitcast_dynamic-update-slice_fusion.8
  2405.4 0.7 copy-done.3
  2406.1 19.7 custom-call.20
  2425.8 5.2 fusion.3
  2431.0 4.2 convolution_subtract_fusion
  2435.2 4.9 fusion.12
  2440.1 25.4 %convolution_bitcast_fusion.2 = f32[4096,256]{0,1:T(8,128)} fusion(bf16[4096,6656]{1,0:T(8,128)(2,1)} %bitcast.133, f32[6656,128]{0,1:T(8,128)} %fusion.12, f32[6656,128]{0,1:T(8,128)S(1)} %bitcast.134), kind=kOutput, calls=%fused_computation.16 | convolution fusion | flops 13965459456 | bytes 65536000 | tf_op jit(solution)/shard_map/dot_general | solution.py:44
  2465.5 5.4 fusion
  2470.8 8.1 copy.31
  2479.0 36.0 %reduce-scatter.8.cloned.1.call-done = f32[512,256]{0,1:T(8,128)} async-done(((f32[4096,256]{0,1:T(8,128)}), f32[512,256]{0,1:T(8,128)}) %reduce-scatter.8.cloned.1.call-update) | async-done | bytes 524304 | tf_op jit(solution)/shard_map/reduce_scatter | solution.py:43
  2514.9 2.0 copy.30
  (84 shorter events, 12.9 us)
Async XLA Ops:
  77.8 1199.1 %all-to-all-start = ((bf16[512,8,6656]{0,2,1:T(8,128)(2,1)}), bf16[512,8,6656]{0,2,1:T(8,128)(2,1)}, u32[]{:S(2)}, u32[]{:S(2)}) async-start(bf16[512,8,6656]{0,2,1:T(8,128)(2,1)} %bitcast.127), calls=%async_computation | async-start | bytes 109051904 | tf_op jit(solution)/shard_map/all_to_all | solution.py:31
  86.6 1254.9 %all-gather.10.cloned.1.call-start = ((), (), s32[]{:S(2)}) async-start(), calls=%async_computation.4 | async-start | bytes 2359296 | tf_op jit(solution)/shard_map/all_gather | solution.py:38
  87.3 1426.5 %all-reduce.5.cloned.1.call-start = ((), (), s32[]{:S(2)}) async-start(), calls=%async_computation.5 | async-start | bytes 13631488 | tf_op jit(solution)/shard_map/psum | solution.py:40
  1367.4 191.8 %all-gather.16.cloned.1.call-start = ((), (), s32[]{:S(2)}) async-start(), calls=%async_computation.13 | async-start | bytes 2359296 | tf_op jit(solution)/shard_map/all_gather | solution.py:27
  1529.9 181.7 %reduce-scatter.4.cloned.1.call-start = ((), (), s32[]{:S(2)}) async-start(), calls=%async_computation.6 | async-start | bytes 4718592 | tf_op jit(solution)/shard_map/reduce_scatter | solution.py:43
  1601.2 0.7 copy-start.4
  1621.5 5.2 copy-start
  1662.1 79.2 %all-gather.12.cloned.1.call-start = ((), (), s32[]{:S(2)}) async-start(), calls=%async_computation.7 | async-start | bytes 2359296 | tf_op jit(solution)/shard_map/all_gather | solution.py:51
  1713.4 199.8 %all-reduce.7.cloned.1.call-start = ((), (), s32[]{:S(2)}) async-start(), calls=%async_computation.8 | async-start | bytes 13631488 | tf_op jit(solution)/shard_map/psum | solution.py:40
  1766.8 195.0 %all-gather.18.cloned.1.call-start = ((), (), s32[]{:S(2)}) async-start(), calls=%async_computation.14 | async-start | bytes 2359296 | tf_op jit(solution)/shard_map/all_gather | solution.py:27
  1932.5 179.9 %reduce-scatter.6.cloned.1.call-start = ((), (), s32[]{:S(2)}) async-start(), calls=%async_computation.9 | async-start | bytes 4718592 | tf_op jit(solution)/shard_map/reduce_scatter | solution.py:43
  2004.4 0.7 copy-start.5
  2024.8 5.2 copy-start.2
  2062.9 79.3 %all-gather.14.cloned.1.call-start = ((), (), s32[]{:S(2)}) async-start(), calls=%async_computation.10 | async-start | bytes 2359296 | tf_op jit(solution)/shard_map/all_gather | solution.py:51
  2114.2 199.9 %all-reduce.9.cloned.1.call-start = ((), (), s32[]{:S(2)}) async-start(), calls=%async_computation.11 | async-start | bytes 13631488 | tf_op jit(solution)/shard_map/psum | solution.py:40
  2167.8 195.0 %all-gather.20.cloned.1.call-start = ((), (), s32[]{:S(2)}) async-start(), calls=%async_computation.15 | async-start | bytes 2359296 | tf_op jit(solution)/shard_map/all_gather | solution.py:27
  2333.5 181.4 %reduce-scatter.8.cloned.1.call-start = ((), (), s32[]{:S(2)}) async-start(), calls=%async_computation.12 | async-start | bytes 4718592 | tf_op jit(solution)/shard_map/reduce_scatter | solution.py:43
  2405.4 0.7 copy-start.3
  2425.8 5.2 copy-start.1
Sparse Core Ops, SparseCore 0:
  89.0 49.5 all-gather.9
  1367.5 146.2 all-reduce.4
  1530.0 29.1 all-gather.15
  1662.2 49.3 reduce-scatter.3
  1713.6 27.6 all-gather.11
  1767.0 146.1 all-reduce.6
  1932.6 29.1 all-gather.17
  2063.1 49.3 reduce-scatter.5
  2114.6 27.6 all-gather.13
  2167.9 146.1 all-reduce.8
  2333.6 29.1 all-gather.19
  2465.6 49.3 reduce-scatter.7
